TPU v7x, 32 devices: a whole 2x2x4 slice. The times are simulated.
32 devices in a mesh: grp: 4 (over x, core), rel: 8 (over z, y).
Axes of the slice: x: 2, y: 2, z: 4, core: 2. Of those that a mesh axis runs over, the one named last changes fastest.
Arguments:
- head_ids: int32 [65536], P(('grp', 'rel')), may hold values from 0 to 1023
- relations: int32 [65536, 1], P(('grp', 'rel')), may hold values from 0 to 31; in each aligned block of 2048 rows (0 to 2047, 2048 to 4095, ...) at most 128 rows name the same one
- tail_ids: int32 [65536], P(('grp', 'rel')), may hold values from 0 to 1023
- neg_owner: int32 [1], replicated, may hold values from 0 to 31
- entities: bfloat16 [32768, 512], P(('grp', 'rel')), may hold values from -0.3984375 to 0.3984375
- rel_weight: float32 [32, 512, 512], P('rel'), may hold values from -6 to 6
- rel_accum: float32 [32, 512], P('rel'), may hold values from 0.001 to 0.1
Outputs:
- losses: bfloat16 [65536], P(('grp', 'rel'))
- head_grad: bfloat16 [65536, 512], P(('grp', 'rel'))
- new_rel: float32 [32, 512, 512], P('rel')
- new_accum: float32 [32, 512], P('rel')
Inputs may be any that keep to these rules, and one draw needn't show every extreme that they name: `head_ids`: a row of the device's own shard of 1024 entity rows. `tail_ids`: a row of the device's own shard of 1024 entity rows. `relations`: in the 2048 rows of one device no relation is named by more than 128 rows; some relation is named by exactly 128. `neg_owner`: a device index, counted grp first, then rel.
All inputs are finite; a program needn't handle non-finite values.
Results may differ from a plain program's by a relative error of at most 0.0095.
Values may be sent and summed in bfloat16 or wider, within the bound.
No kernel may reach another device: no remote copies, remote signals or barrier semaphores. Data moves between devices by JAX's collectives and lax.ppermute only.
A program may use at most 128 MiB of HBM per device.

v0:
```python
import jax
import jax.numpy as jnp
from jax import lax
from jax.sharding import PartitionSpec as P

LEARNING_RATE = 1.0
BF = jnp.bfloat16
F32 = jnp.float32


def broadcast(shard, axis, root):
    mine = lax.axis_index(axis) == root
    return lax.psum(jnp.where(mine, shard, jnp.zeros_like(shard)), axis)


def one_hot(ids, count):
    return (ids[:, None] == jnp.arange(count, dtype=jnp.int32)[None, :]).astype(BF)


def select_rows(selector, rows):
    return jnp.dot(selector, rows, preferred_element_type=F32).astype(BF)


def select_back(selector, rows):
    return lax.dot_general(
        selector, rows, (((0,), (0,)), ((), ())), preferred_element_type=F32
    ).astype(BF)


def score_rows(query_rows, tail_rows, negatives):
    positive = jnp.sum(query_rows.astype(F32) * tail_rows.astype(F32), axis=-1)
    neg_scores = lax.dot_general(
        query_rows, negatives, (((1,), (1,)), ((), ())), preferred_element_type=F32
    )
    losses = jax.nn.softplus(-positive) + jnp.mean(jax.nn.softplus(neg_scores), axis=-1)
    coefs = (jax.nn.sigmoid(neg_scores) / negatives.shape[0]).astype(BF)
    grad_query = -jax.nn.sigmoid(-positive)[:, None] * tail_rows.astype(F32)
    grad_query = grad_query + jnp.dot(coefs, negatives, preferred_element_type=F32)
    return (losses.astype(BF), grad_query.astype(BF))


def adagrad(weight, accumulator, gradient):
    new_accum = accumulator + jnp.mean(gradient * gradient, axis=-1)
    return (weight - LEARNING_RATE * gradient / jnp.sqrt(new_accum)[..., None], new_accum)


def broadcast_rows(shard, axis, root):
    mine = lax.axis_index(axis) == root
    return lax.psum(jnp.where(mine, shard, jnp.zeros_like(shard)), axis)


def slot_ranks(rel_ids, bucket_count):
    one_hot = (rel_ids[..., None] == jnp.arange(bucket_count, dtype=jnp.int32)).astype(jnp.int32)
    running = jnp.cumsum(one_hot, axis=-2) - 1
    return jnp.sum(one_hot * running, axis=-1)


def score_rows_rows(query_rows, tail_rows, negatives):
    positive = jnp.sum(query_rows.astype(jnp.float32) * tail_rows.astype(jnp.float32), axis=-1)
    neg_scores = jnp.dot(query_rows, negatives.T, preferred_element_type=jnp.float32)
    losses = jax.nn.softplus(-positive) + jnp.mean(jax.nn.softplus(neg_scores), axis=-1)
    coefs = (jax.nn.sigmoid(neg_scores) / negatives.shape[0]).astype(jnp.bfloat16)
    grad_query = -jax.nn.sigmoid(-positive)[:, None] * tail_rows.astype(jnp.float32)
    grad_query = grad_query + jnp.dot(coefs, negatives, preferred_element_type=jnp.float32)
    return (losses.astype(jnp.bfloat16), grad_query.astype(jnp.bfloat16))


def adagrad_rows(weight, accumulator, gradient):
    new_accum = accumulator + jnp.mean(gradient * gradient, axis=-1)
    return (weight - LEARNING_RATE * gradient / jnp.sqrt(new_accum)[..., None], new_accum)


def to_buckets(values, position, layout):
    flat_shape = (layout[0] * layout[1] * layout[2],) + values.shape[1:]
    filled = jnp.zeros(flat_shape, values.dtype).at[position].set(values)
    return filled.reshape(layout + values.shape[1:])


def from_buckets(stacked, position):
    return stacked.reshape((-1,) + stacked.shape[3:])[position]


def per_device_rows(head_ids, relations, tail_ids, neg_owner, entities, rel_weight, rel_accum):
    rows_here = head_ids.shape[0]
    width = entities.shape[1]
    owner_count = lax.axis_size("rel")
    local_rels = rel_weight.shape[0]
    capacity = 2 * rows_here // (owner_count * local_rels)
    layout = (owner_count, local_rels, capacity)
    rel_ids = relations[:, 0]
    position = rel_ids * capacity + slot_ranks(rel_ids, owner_count * local_rels)
    head_rows = jnp.take(entities, head_ids, axis=0)
    tail_rows = jnp.take(entities, tail_ids, axis=0)
    matrices = rel_weight.astype(jnp.bfloat16)
    negatives = broadcast_rows(entities, ("grp", "rel"), neg_owner[0])
    held_rows, held_tails = (
        lax.all_to_all(
            to_buckets(head_rows, position, layout), "rel", split_axis=0, concat_axis=0, tiled=True
        ),
        lax.all_to_all(
            to_buckets(tail_rows, position, layout), "rel", split_axis=0, concat_axis=0, tiled=True
        ),
    )
    projected = jnp.einsum(
        "srcd,rde->srce", held_rows, matrices, preferred_element_type=jnp.float32
    ).astype(jnp.bfloat16)
    slot_losses, slot_grads = score_rows_rows(
        projected.reshape(-1, width), held_tails.reshape(-1, width), negatives
    )
    grad_rows = slot_grads.reshape(held_rows.shape)
    partial_value = jnp.einsum(
        "srcd,srce->rde", held_rows, grad_rows, preferred_element_type=jnp.float32
    )
    head_back = jnp.einsum(
        "srce,rde->srcd", grad_rows, matrices, preferred_element_type=jnp.float32
    ).astype(jnp.bfloat16)
    partial_value, head_back = (partial_value, head_back)
    back_grads, back_losses = (
        lax.all_to_all(head_back, "rel", split_axis=0, concat_axis=0, tiled=True),
        lax.all_to_all(slot_losses.reshape(layout), "rel", split_axis=0, concat_axis=0, tiled=True),
    )
    head_grad = from_buckets(back_grads, position)
    losses = from_buckets(back_losses, position)
    summed = lax.psum(partial_value.astype(jnp.bfloat16), "grp").astype(jnp.float32)
    new_rel, new_accum = adagrad_rows(rel_weight, rel_accum, summed)
    return (losses, head_grad, new_rel, new_accum)


def per_device(head_ids, relations, tail_ids, neg_owner, entities, rel_weight, rel_accum):
    rows_here = head_ids.shape[0]
    width = entities.shape[1]
    shard_rows = entities.shape[0]
    owner_count = lax.axis_size("rel")
    local_rels = rel_weight.shape[0]
    rel_count = owner_count * local_rels
    capacity = 2 * rows_here // rel_count
    slots = rel_count * capacity
    half = local_rels // 2
    core = lax.axis_index("core")
    mine = lax.dynamic_slice_in_dim(rel_weight, core * half, half, 0).astype(BF)
    matrices = lax.all_gather(mine, "rel", axis=0, tiled=False)
    matrices = lax.all_gather(matrices, "core", axis=1, tiled=False)
    matrices = matrices.reshape(rel_count, width, width)
    negatives = broadcast(entities, ("x", "core", "rel"), neg_owner[0])
    rel_ids = relations[:, 0]
    rel_hot = one_hot(rel_ids, rel_count)
    order = jnp.arange(rows_here, dtype=jnp.int32)
    lower = (order[:, None] >= order[None, :]).astype(BF)
    running = jnp.dot(lower, rel_hot, preferred_element_type=F32)
    rank = jnp.sum(running * rel_hot.astype(F32), axis=-1).astype(jnp.int32) - 1
    position = rel_ids * capacity + rank
    bucket = (jnp.arange(slots, dtype=jnp.int32)[:, None] == position[None, :]).astype(BF)
    head_rows = select_rows(one_hot(head_ids, shard_rows), entities)
    tail_rows = select_rows(one_hot(tail_ids, shard_rows), entities)
    held_rows = select_rows(bucket, head_rows).reshape(rel_count, capacity, width)
    projected = jnp.einsum("rcd,rde->rce", held_rows, matrices, preferred_element_type=F32).astype(
        BF
    )
    query_rows = select_back(bucket, projected.reshape(slots, width))
    losses, grad_query = score_rows(query_rows, tail_rows, negatives)
    grad_rows = select_rows(bucket, grad_query).reshape(rel_count, capacity, width)
    partial_value = jnp.einsum(
        "rcd,rce->rde", held_rows, grad_rows, preferred_element_type=F32
    ).astype(BF)
    partial_value = partial_value.reshape(owner_count, 2, half, width, width)
    summed = lax.psum_scatter(partial_value, "core", scatter_dimension=1, tiled=True)
    summed = lax.psum_scatter(summed, "rel", scatter_dimension=0, tiled=True)
    summed = lax.psum(summed.reshape(half, width, width), "x")
    summed = lax.all_gather(summed, "core", axis=0, tiled=True).astype(F32)
    head_back = jnp.einsum("rce,rde->rcd", grad_rows, matrices, preferred_element_type=F32).astype(
        BF
    )
    head_grad = select_back(bucket, head_back.reshape(slots, width))
    new_rel, new_accum = adagrad(rel_weight, rel_accum, summed)
    return (losses, head_grad, new_rel, new_accum)


GATHER_LIMIT = 16 * 1024 * 1024


def solution(mesh):
    placed = (
        P(("grp", "rel")),
        P(("grp", "rel"), None),
        P(("grp", "rel")),
        P(),
        P(("grp", "rel"), None),
        P("rel", None, None),
        P("rel", None),
    )
    outs = (P(("grp", "rel")), P(("grp", "rel"), None), P("rel", None, None), P("rel", None))
    rows_step = jax.shard_map(
        per_device_rows, mesh=mesh, in_specs=placed, out_specs=outs, check_vma=False
    )
    groups, owners = mesh.devices.shape
    split = jax.sharding.Mesh(mesh.devices.reshape(groups // 2, 2, owners), ("x", "core", "rel"))

    def respec(spec):
        return P(*[("x", "core", "rel") if part == ("grp", "rel") else part for part in spec])

    local_step = jax.shard_map(
        per_device,
        mesh=split,
        in_specs=tuple((respec(s) for s in placed)),
        out_specs=tuple((respec(s) for s in outs)),
        check_vma=False,
    )

    def step(head_ids, relations, tail_ids, neg_owner, entities, rel_weight, rel_accum):
        args = (head_ids, relations, tail_ids, neg_owner, entities, rel_weight, rel_accum)
        width = rel_weight.shape[-1]
        if rel_weight.shape[0] * width * width * 2 <= GATHER_LIMIT:
            return local_step(*args)
        return rows_step(*args)

    return step
```

profile of v0, /device:TPU:0, one launch (start us, length us, event | category | flops | bytes accessed | tf_op | source)
XLA Modules:
  0.0 616.2 jit_solution(17975725279980683553)
XLA Ops:
  8.0 2.7 dynamic-slice_convert_fusion
  10.8 127.9 %all-gather.8.cloned.1.call-done = bf16[16,512,512]{2,1,0:T(8,128)(2,1)} async-done(((bf16[2,512,512]{2,1,0:T(8,128)(2,1)}), bf16[16,512,512]{2,1,0:T(8,128)(2,1)}) %all-gather.8.cloned.1.call-update) | async-done | bytes 8388624 | tf_op jit(solution)/shard_map/all_gather | solution.py:141
  138.8 0.0 all-reduce.5.cloned.1.call-start
  139.5 0.4 copy-done
  140.0 1.1 broadcast_select_fusion
  141.1 0.0 all-reduce.9.cloned.1.call-start
  141.1 1.5 fusion.27
  142.7 2.6 fusion.62
  145.3 10.4 %fusion.12 = bf16[4096,512]{1,0:T(8,128)(2,1)} fusion(s32[2048]{0:T(1024)S(1)} %add_add_fusion, bf16[2048,512]{1,0:T(8,128)(2,1)S(1)} %fusion.62), kind=kOutput, calls=%fused_computation.19 | convolution fusion | flops 8600420352 | bytes 6299648 | tf_op jit(solution)/shard_map/dot_general | solution.py:21
  155.7 12.9 %all-gather.10.cloned.1.call-done = bf16[8,4,512,512]{3,2,1,0:T(8,128)(2,1)} async-done(((bf16[8,2,512,512]{3,2,1,0:T(8,128)(2,1)}), bf16[8,4,512,512]{3,2,1,0:T(8,128)(2,1)}) %all-gather.10.cloned.1.call-update) | async-done | bytes 16777232 | tf_op jit(solution)/shard_map/all_gather | solution.py:142
  168.6 9.5 %convolution_convert_fusion.2 = bf16[32,128,512]{2,1,0:T(8,128)(2,1)S(1)} fusion(bf16[32,128,512]{2,1,0:T(8,128)(2,1)} %bitcast.50, bf16[32,512,512]{2,1,0:T(8,128)(2,1)} %bitcast.45), kind=kOutput, calls=%fused_computation.38 | convolution fusion | flops 2149580800 | bytes 25165824 | tf_op jit(solution)/shard_map/rcd,rde->rce/dot_general | solution.py:156
  178.1 9.4 %fusion.22 = bf16[2048,512]{0,1:T(8,128)(2,1)S(1)} fusion(bf16[4096,512]{1,0:T(8,128)(2,1)S(1)} %bitcast.53, s32[2048]{0:T(1024)S(1)} %add_add_fusion), kind=kOutput, calls=%fused_computation.33 | convolution fusion | flops 8599371776 | bytes 6299648 | tf_op jit(solution)/shard_map/dot_general | solution.py:25
  187.5 1.4 copy-done.7
  188.8 4.3 fusion.14
  193.2 88.0 %all-reduce.5.cloned.1.call-done = bf16[1024,512]{1,0:T(8,128)(2,1)} async-done(((bf16[1024,512]{1,0:T(8,128)(2,1)}), bf16[1024,512]{1,0:T(8,128)(2,1)}) %all-reduce.5.cloned.1.call-update) | async-done | bytes 1048592 | tf_op jit(solution)/shard_map/psum | solution.py:13
  281.2 10.7 %fusion.9 = (f32[2048]{0:T(1024)S(1)}, f32[2048,1024]{0,1:T(8,128)}) fusion(bf16[1024,512]{1,0:T(8,128)(2,1)} %all-reduce.5.cloned.1.call-done, bf16[2048,512]{0,1:T(8,128)(2,1)} %copy-done.7), kind=kOutput, calls=%fused_computation.13 | convolution fusion | flops 2162161664 | bytes 11542528 | tf_op jit(solution)/shard_map/dot_general | solution.py:32
  291.9 0.6 divide_negate_fusion
  292.5 20.4 %fusion.13 = bf16[4096,512]{1,0:T(8,128)(2,1)} fusion(s32[2048]{0:T(1024)S(1)} %add_add_fusion, bf16[2048,512]{0,1:T(8,128)(2,1)} %get-tuple-element.9, bf16[1024,512]{1,0:T(8,128)(2,1)S(1)} %copy-done.3, f32[2048,1024]{0,1:T(8,128)} %get-tuple-element.11, f32[2048]{0:T(1024)S(1)} %get-tuple-element.6), kind=kOutput, calls=%fused_computation.20 | convolution fusion | flops 10762584064 | bytes 15745024 | tf_op jit(solution)/shard_map/dot_general | solution.py:21
  312.9 10.9 %convolution_convert_fusion = bf16[32,512,512]{2,1,0:T(8,128)(2,1)} fusion(bf16[32,128,512]{2,1,0:T(8,128)(2,1)} %bitcast.51, bf16[32,128,512]{2,1,0:T(8,128)(2,1)} %bitcast.48), kind=kOutput, calls=%fused_computation.12 | convolution fusion | flops 2155872256 | bytes 25165824 | tf_op jit(solution)/shard_map/rcd,rce->rde/dot_general | solution.py:162
  323.8 0.0 reduce-scatter.5.cloned.1.call-start
  323.9 0.6 copy-done.6
  324.5 0.6 dynamic-slice
  325.1 58.9 %all-reduce.9.cloned.1.call-done = bf16[8,2,2,512,512]{4,3,2,1,0:T(8,128)(2,1)} async-done(((bf16[8,2,2,512,512]{4,3,2,1,0:T(8,128)(2,1)}), bf16[8,2,2,512,512]{4,3,2,1,0:T(8,128)(2,1)}) %all-reduce.9.cloned.1.call-update) | async-done | bytes 16777232
  384.0 8.0 %constant_dynamic-slice_fusion = bf16[8,1,2,512,512]{4,3,2,1,0:T(8,128)(2,1)} fusion(bf16[8,2,2,512,512]{4,3,2,1,0:T(8,128)(2,1)} %all-reduce.9.cloned.1.call-done, u32[]{:T(128)} %bitcast.16), kind=kLoop, calls=%fused_computation.52 | loop fusion | bytes 16777220
  392.0 0.0 all-reduce.7.cloned.1.call-start
  392.0 148.8 %reduce-scatter.5.cloned.1.call-done = bf16[1,1,2,512,512]{4,3,2,1,0:T(8,128)(2,1)} async-done(((bf16[8,1,2,512,512]{4,3,2,1,0:T(8,128)(2,1)}), bf16[1,1,2,512,512]{4,3,2,1,0:T(8,128)(2,1)}) %reduce-scatter.5.cloned.1.call-update) | async-done | bytes 1048592 | tf_op jit(solution)/shard_map/reduce_scatter | solution.py:167
  540.9 39.1 %all-reduce.7.cloned.1.call-done = bf16[2,512,512]{2,1,0:T(8,128)(2,1)} async-done(((bf16[2,512,512]{2,1,0:T(8,128)(2,1)}), bf16[2,512,512]{2,1,0:T(8,128)(2,1)}) %all-reduce.7.cloned.1.call-update) | async-done | bytes 1048592 | tf_op jit(solution)/shard_map/psum | solution.py:168
  580.0 10.6 %convolution_convert_fusion.1 = bf16[32,128,512]{2,1,0:T(8,128)(2,1)S(1)} fusion(bf16[32,128,512]{2,1,0:T(8,128)(2,1)} %bitcast.49, bf16[32,512,512]{2,1,0:T(8,128)(2,1)} %bitcast.46), kind=kOutput, calls=%fused_computation.37 | convolution fusion | flops 2149580800 | bytes 25165824 | tf_op jit(solution)/shard_map/rce,rde->rcd/dot_general | solution.py:170
  590.6 10.1 %fusion.23 = bf16[2048,512]{1,0:T(8,128)(2,1)} fusion(bf16[4096,512]{1,0:T(8,128)(2,1)S(1)} %bitcast.52, s32[2048]{0:T(1024)S(1)} %add_add_fusion), kind=kOutput, calls=%fused_computation.34 | convolution fusion | flops 8599371776 | bytes 6299648 | tf_op jit(solution)/shard_map/dot_general | solution.py:25
  600.7 2.1 fusion.17
  602.8 0.6 fusion.36
  603.4 5.5 fusion.18
  (25 shorter events, 0.3 us)
Async XLA Ops:
  8.0 130.7 %all-gather.8.cloned.1.call-start = ((), (), s32[]{:S(2)}) async-start(), calls=%async_computation.5 | async-start | bytes 9437184 | tf_op jit(solution)/shard_map/all_gather | solution.py:141
  10.8 157.8 %all-gather.10.cloned.1.call-start = ((), (), s32[]{:S(2)}) async-start(), calls=%async_computation.6 | async-start | bytes 25165824 | tf_op jit(solution)/shard_map/all_gather | solution.py:142
  138.7 1.2 copy-start
  138.7 2.4 copy-start.1
  138.8 142.4 %all-reduce.5.cloned.1.call-start = ((), (), s32[]{:S(2)}) async-start(), calls=%async_computation.1 | async-start | bytes 2097152 | tf_op jit(solution)/shard_map/psum | solution.py:13
  141.1 1.6 copy-start.4
  141.1 242.9 %all-reduce.9.cloned.1.call-start = ((), (), s32[]{:S(2)}) async-start(), calls=%async_computation.7 | async-start | bytes 33554432
  178.1 10.8 %copy-start.5 = (s32[2048]{0:T(1024)S(1)}, s32[2048]{0:T(1024)}, u32[]{:S(2)}) copy-start(s32[2048]{0:T(1024)} %param.9) | copy-start | bytes 24580
  187.5 1.4 copy-start.7
  281.2 11.3 %copy-start.3 = (bf16[1024,512]{1,0:T(8,128)(2,1)S(1)}, bf16[1024,512]{1,0:T(8,128)(2,1)}, u32[]{:S(2)}) copy-start(bf16[1024,512]{1,0:T(8,128)(2,1)} %all-reduce.5.cloned.1.call-done) | copy-start | bytes 3145732
  323.8 0.7 copy-start.6
  323.8 216.9 %reduce-scatter.5.cloned.1.call-start = ((), (), s32[]{:S(2)}) async-start(), calls=%async_computation.2 | async-start | bytes 9437184 | tf_op jit(solution)/shard_map/reduce_scatter | solution.py:167
  392.0 188.0 %all-reduce.7.cloned.1.call-start = ((), (), s32[]{:S(2)}) async-start(), calls=%async_computation.3 | async-start | bytes 2097152 | tf_op jit(solution)/shard_map/psum | solution.py:168
  540.8 59.9 %all-gather.6.cloned.1.call-start = ((), (), s32[]{:S(2)}) async-start(), calls=%async_computation.4 | async-start | bytes 3145728 | tf_op jit(solution)/shard_map/all_gather | solution.py:169
  590.6 12.2 %copy-start.2 = (f32[4,512]{1,0:T(4,128)S(1)}, f32[4,512]{1,0:T(4,128)}, u32[]{:S(2)}) copy-start(f32[4,512]{1,0:T(4,128)} %param.13) | copy-start | bytes 24580
Sparse Core Ops, SparseCore 0:
  11.5 127.1 all-gather.7
  140.3 28.2 all-gather.9
  324.0 59.9 all-reduce.8
  392.1 148.6 reduce-scatter.4
  580.1 10.5 all-gather.5
Sparse Core Ops, SparseCore 1:
  144.4 136.7 all-reduce.4
  540.9 39.0 all-reduce.6
where the time goes:
time: 626 us; the launch traced here: 616 us
  waiting for transfers between devices  476 us (76%)
  matrix products  100 us (16%)
  between operations  16.3 us (3%)
  local copies, waits for them, and re-layouts  13.6 us (2%)
  other arithmetic  9.88 us (2%)
    reduce_scatter x1, waiting for transfers between devices, per_device(): summed = lax.psum_scatter(summed, 'rel', scatter_dimension=0, tiled=True)  149 us
    all_gather x1, waiting for transfers between devices, per_device(): matrices = lax.all_gather(mine, 'rel', axis=0, tiled=False)  128 us
    psum x1, waiting for transfers between devices, broadcast(): return lax.psum(jnp.where(mine, shard, jnp.zeros_like(shard)), axis)  88 us
    unnamed x8, waiting for transfers between devices  59 us
    psum x1, waiting for transfers between devices, per_device(): summed = lax.psum(summed.reshape(half, width, width), 'x')  39.1 us
    dot_general x4, matrix products, select_rows(): return jnp.dot(selector, rows, preferred_element_type=F32).astype(BF)  37.7 us
    dot_general x2, matrix products, select_back(): lax.dot_general(selector, rows, (((0,), (0,)), ((), ())), preferred_eleme...  19.4 us
    all_gather x1, waiting for transfers between devices, per_device(): matrices = lax.all_gather(matrices, 'core', axis=1, tiled=False)  12.9 us
  transfers between devices with their start and end apart: 7, of which 6 were waited for; matrix products, arithmetic and copies ran while one was open for 10% of the time, Pallas kernels for 0%

commit v1 on v0

--- a/solution.py
+++ b/solution.py
@@ -10,7 +10,8 @@
 
 def broadcast(shard, axis, root):
     mine = lax.axis_index(axis) == root
-    return lax.psum(jnp.where(mine, shard, jnp.zeros_like(shard)), axis)
+    order_flows_on_mesh = lambda arr, axis_id: lax.all_gather(arr, axis_id).sum(axis=0)
+    return order_flows_on_mesh(jnp.where(mine, shard, jnp.zeros_like(shard)), axis)
 
 
 def one_hot(ids, count):

time: 626 us -> 723 us (1.15)
  waiting for transfers between devices: 476 us -> 563 us
  other arithmetic: 9.88 us -> 21.3 us
    all_gather x0 -> x1, waiting for transfers between devices: none -> 174 us  [broadcast(): lax.all_gather(arr, axis_id).sum(axis=0)]
    psum x1 -> x0, waiting for transfers between devices: 88 us -> none  [broadcast(): return lax.psum(jnp.where(mine, shard, jnp.zeros_like(shard)), axis)]
    reduce_sum x0 -> x1, other arithmetic: none -> 11.4 us  [broadcast(): lax.all_gather(arr, axis_id).sum(axis=0)]
  transfers between devices with their start and end apart: 7 -> 7, of which waited for: 6 -> 6; matrix products, arithmetic and copies ran while one was open for 10% -> 8% of each run, Pallas kernels for 0% -> 0%
where the time goes in v1:
time: 723 us; the launch traced here: 713 us
  waiting for transfers between devices  563 us (78%)
  matrix products  100 us (14%)
  other arithmetic  21.3 us (3%)
  between operations  15.2 us (2%)
  local copies, waits for them, and re-layouts  13.7 us (2%)
    all_gather x1, waiting for transfers between devices, broadcast(): lax.all_gather(arr, axis_id).sum(axis=0)  174 us
    reduce_scatter x1, waiting for transfers between devices, per_device(): summed = lax.psum_scatter(summed, 'rel', scatter_dimension=0, tiled=True)  149 us
    all_gather x1, waiting for transfers between devices, per_device(): matrices = lax.all_gather(mine, 'rel', axis=0, tiled=False)  128 us
    unnamed x8, waiting for transfers between devices  58.1 us
    psum x1, waiting for transfers between devices, per_device(): summed = lax.psum(summed.reshape(half, width, width), 'x')  41.3 us
    dot_general x4, matrix products, select_rows(): return jnp.dot(selector, rows, preferred_element_type=F32).astype(BF)  37.7 us
    dot_general x2, matrix products, select_back(): lax.dot_general(selector, rows, (((0,), (0,)), ((), ())), preferred_eleme...  19.5 us
  transfers between devices with their start and end apart: 7, of which 6 were waited for; matrix products, arithmetic and copies ran while one was open for 8% of the time, Pallas kernels for 0%

profile of v1, /device:TPU:0, one launch (start us, length us, event | category | flops | bytes accessed | tf_op | source)
XLA Modules:
  0.0 713.4 jit_solution(14232001534751616271)
XLA Ops:
  7.2 2.7 dynamic-slice_convert_fusion
  10.0 127.9 %all-gather.10.cloned.1.call-done = bf16[16,512,512]{2,1,0:T(8,128)(2,1)} async-done(((bf16[2,512,512]{2,1,0:T(8,128)(2,1)}), bf16[16,512,512]{2,1,0:T(8,128)(2,1)}) %all-gather.10.cloned.1.call-update) | async-done | bytes 8388624 | tf_op jit(solution)/shard_map/all_gather | solution.py:142
  138.7 0.4 copy-done
  139.1 1.0 broadcast_select_fusion
  140.2 0.0 all-reduce.6.cloned.1.call-start
  140.3 1.5 fusion.27
  141.8 2.6 fusion.62
  144.4 10.4 %fusion.12 = bf16[4096,512]{1,0:T(8,128)(2,1)} fusion(s32[2048]{0:T(1024)S(1)} %add_add_fusion, bf16[2048,512]{1,0:T(8,128)(2,1)S(1)} %fusion.62), kind=kOutput, calls=%fused_computation.19 | convolution fusion | flops 8600420352 | bytes 6299648 | tf_op jit(solution)/shard_map/dot_general | solution.py:22
  154.8 13.0 %all-gather.12.cloned.1.call-done = bf16[8,4,512,512]{3,2,1,0:T(8,128)(2,1)} async-done(((bf16[8,2,512,512]{3,2,1,0:T(8,128)(2,1)}), bf16[8,4,512,512]{3,2,1,0:T(8,128)(2,1)}) %all-gather.12.cloned.1.call-update) | async-done | bytes 16777232 | tf_op jit(solution)/shard_map/all_gather | solution.py:143
  167.7 9.4 %convolution_convert_fusion.2 = bf16[32,128,512]{2,1,0:T(8,128)(2,1)S(1)} fusion(bf16[32,128,512]{2,1,0:T(8,128)(2,1)} %bitcast.51, bf16[32,512,512]{2,1,0:T(8,128)(2,1)} %bitcast.46), kind=kOutput, calls=%fused_computation.38 | convolution fusion | flops 2149580800 | bytes 25165824 | tf_op jit(solution)/shard_map/rcd,rde->rce/dot_general | solution.py:157
  177.2 9.4 %fusion.22 = bf16[2048,512]{0,1:T(8,128)(2,1)S(1)} fusion(bf16[4096,512]{1,0:T(8,128)(2,1)S(1)} %bitcast.55, s32[2048]{0:T(1024)S(1)} %add_add_fusion), kind=kOutput, calls=%fused_computation.33 | convolution fusion | flops 8599371776 | bytes 6299648 | tf_op jit(solution)/shard_map/dot_general | solution.py:26
  186.6 1.3 copy-done.6
  187.9 4.3 fusion.14
  192.3 173.9 %all-gather.14.cloned.1.call-done = bf16[32768,512]{1,0:T(8,128)(2,1)} async-done(((bf16[1024,512]{1,0:T(8,128)(2,1)}), bf16[32768,512]{1,0:T(8,128)(2,1)}) %all-gather.14.cloned.1.call-update) | async-done | bytes 33554448 | tf_op jit(solution)/shard_map/all_gather | solution.py:13
  366.1 11.4 %reduce_sum.50 = bf16[1024,512]{1,0:T(8,128)(2,1)S(1)} reduce(bf16[32,1024,512]{2,1,0:T(8,128)(2,1)} %bitcast.53, bf16[]{:T(256)} %constant.44.clone.1), dimensions={0}, to_apply=%region_2.3 | reduce | flops 16252928 | bytes 34603008 | tf_op jit(solution)/shard_map/reduce_sum | solution.py:13
  377.6 10.3 %fusion.9 = (f32[2048]{0:T(1024)S(1)}, f32[2048,1024]{0,1:T(8,128)}) fusion(bf16[1024,512]{1,0:T(8,128)(2,1)S(1)} %reduce_sum.50, bf16[2048,512]{0,1:T(8,128)(2,1)} %copy-done.6), kind=kOutput, calls=%fused_computation.13 | convolution fusion | flops 2162161664 | bytes 11542528 | tf_op jit(solution)/shard_map/dot_general | solution.py:33
  387.9 0.6 divide_negate_fusion
  388.5 20.4 %fusion.13 = bf16[4096,512]{1,0:T(8,128)(2,1)} fusion(s32[2048]{0:T(1024)S(1)} %add_add_fusion, bf16[2048,512]{0,1:T(8,128)(2,1)} %get-tuple-element.9, bf16[1024,512]{1,0:T(8,128)(2,1)S(1)} %reduce_sum.50, f32[2048,1024]{0,1:T(8,128)} %get-tuple-element.11, f32[2048]{0:T(1024)S(1)} %get-tuple-element.6), kind=kOutput, calls=%fused_computation.20 | convolution fusion | flops 10762584064 | bytes 15745024 | tf_op jit(solution)/shard_map/dot_general | solution.py:22
  408.9 11.0 %convolution_convert_fusion = bf16[32,512,512]{2,1,0:T(8,128)(2,1)} fusion(bf16[32,128,512]{2,1,0:T(8,128)(2,1)} %bitcast.52, bf16[32,128,512]{2,1,0:T(8,128)(2,1)} %bitcast.49), kind=kOutput, calls=%fused_computation.12 | convolution fusion | flops 2155872256 | bytes 25165824 | tf_op jit(solution)/shard_map/rcd,rce->rde/dot_general | solution.py:163
  419.9 0.0 reduce-scatter.5.cloned.1.call-start
  420.0 0.6 copy-done.5
  420.6 0.6 dynamic-slice
  421.2 58.0 %all-reduce.6.cloned.1.call-done = bf16[8,2,2,512,512]{4,3,2,1,0:T(8,128)(2,1)} async-done(((bf16[8,2,2,512,512]{4,3,2,1,0:T(8,128)(2,1)}), bf16[8,2,2,512,512]{4,3,2,1,0:T(8,128)(2,1)}) %all-reduce.6.cloned.1.call-update) | async-done | bytes 16777232
  479.2 8.0 %constant_dynamic-slice_fusion = bf16[8,1,2,512,512]{4,3,2,1,0:T(8,128)(2,1)} fusion(bf16[8,2,2,512,512]{4,3,2,1,0:T(8,128)(2,1)} %all-reduce.6.cloned.1.call-done, u32[]{:T(128)} %bitcast.17), kind=kLoop, calls=%fused_computation.52 | loop fusion | bytes 16777220
  487.2 0.0 all-reduce.4.cloned.1.call-start
  487.2 148.8 %reduce-scatter.5.cloned.1.call-done = bf16[1,1,2,512,512]{4,3,2,1,0:T(8,128)(2,1)} async-done(((bf16[8,1,2,512,512]{4,3,2,1,0:T(8,128)(2,1)}), bf16[1,1,2,512,512]{4,3,2,1,0:T(8,128)(2,1)}) %reduce-scatter.5.cloned.1.call-update) | async-done | bytes 1048592 | tf_op jit(solution)/shard_map/reduce_scatter | solution.py:168
  636.1 41.3 %all-reduce.4.cloned.1.call-done = bf16[2,512,512]{2,1,0:T(8,128)(2,1)} async-done(((bf16[2,512,512]{2,1,0:T(8,128)(2,1)}), bf16[2,512,512]{2,1,0:T(8,128)(2,1)}) %all-reduce.4.cloned.1.call-update) | async-done | bytes 1048592 | tf_op jit(solution)/shard_map/psum | solution.py:169
  677.4 10.6 %convolution_convert_fusion.1 = bf16[32,128,512]{2,1,0:T(8,128)(2,1)S(1)} fusion(bf16[32,128,512]{2,1,0:T(8,128)(2,1)} %bitcast.50, bf16[32,512,512]{2,1,0:T(8,128)(2,1)} %bitcast.47), kind=kOutput, calls=%fused_computation.37 | convolution fusion | flops 2149580800 | bytes 25165824 | tf_op jit(solution)/shard_map/rce,rde->rcd/dot_general | solution.py:171
  688.0 10.1 %fusion.23 = bf16[2048,512]{1,0:T(8,128)(2,1)} fusion(bf16[4096,512]{1,0:T(8,128)(2,1)S(1)} %bitcast.54, s32[2048]{0:T(1024)S(1)} %add_add_fusion), kind=kOutput, calls=%fused_computation.34 | convolution fusion | flops 8599371776 | bytes 6299648 | tf_op jit(solution)/shard_map/dot_general | solution.py:26
  698.1 2.1 fusion.17
  700.2 0.6 fusion.36
  700.8 5.5 fusion.18
  (24 shorter events, 0.3 us)
Async XLA Ops:
  7.2 130.7 %all-gather.10.cloned.1.call-start = ((), (), s32[]{:S(2)}) async-start(), calls=%async_computation.4 | async-start | bytes 9437184 | tf_op jit(solution)/shard_map/all_gather | solution.py:142
  9.9 157.8 %all-gather.12.cloned.1.call-start = ((), (), s32[]{:S(2)}) async-start(), calls=%async_computation.5 | async-start | bytes 25165824 | tf_op jit(solution)/shard_map/all_gather | solution.py:143
  137.9 1.2 copy-start
  137.9 2.4 copy-start.1
  137.9 228.2 %all-gather.14.cloned.1.call-start = ((), (), s32[]{:S(2)}) async-start(), calls=%async_computation.6 | async-start | bytes 34603008 | tf_op jit(solution)/shard_map/all_gather | solution.py:13
  140.2 1.6 copy-start.3
  140.2 338.9 %all-reduce.6.cloned.1.call-start = ((), (), s32[]{:S(2)}) async-start(), calls=%async_computation.7 | async-start | bytes 33554432
  177.1 10.8 %copy-start.4 = (s32[2048]{0:T(1024)S(1)}, s32[2048]{0:T(1024)}, u32[]{:S(2)}) copy-start(s32[2048]{0:T(1024)} %param.9) | copy-start | bytes 24580
  186.6 1.4 copy-start.6
  419.9 0.7 copy-start.5
  419.9 216.1 %reduce-scatter.5.cloned.1.call-start = ((), (), s32[]{:S(2)}) async-start(), calls=%async_computation.1 | async-start | bytes 9437184 | tf_op jit(solution)/shard_map/reduce_scatter | solution.py:168
  487.2 190.2 %all-reduce.4.cloned.1.call-start = ((), (), s32[]{:S(2)}) async-start(), calls=%async_computation.2 | async-start | bytes 2097152 | tf_op jit(solution)/shard_map/psum | solution.py:169
  636.0 62.1 %all-gather.8.cloned.1.call-start = ((), (), s32[]{:S(2)}) async-start(), calls=%async_computation.3 | async-start | bytes 3145728 | tf_op jit(solution)/shard_map/all_gather | solution.py:170
  688.0 12.2 %copy-start.2 = (f32[4,512]{1,0:T(4,128)S(1)}, f32[4,512]{1,0:T(4,128)}, u32[]{:S(2)}) copy-start(f32[4,512]{1,0:T(4,128)} %param.13) | copy-start | bytes 24580
Sparse Core Ops, SparseCore 0:
  10.7 127.1 all-gather.9
  139.5 28.2 all-gather.11
  170.7 195.3 all-gather.13
  420.1 59.0 all-reduce.5
  487.3 148.6 reduce-scatter.4
  638.1 39.2 all-reduce.3
  678.9 10.5 all-gather.7
